TPU v7x, 256 devices: a whole 4x4x8 slice. The times are simulated.
256 devices in a mesh: section: 16 (over y_lo, x, core), expert: 16 (over z, y_hi).
Axes of the slice: x: 4, y: 4 (y_hi: 2, y_lo: 2; y = y_hi * 2 + y_lo), z: 8, core: 2. Of those that a mesh axis runs over, the one named last changes fastest.
Arguments:
- activations: bfloat16 [16384, 8192], P('section', 'expert'), may hold values from -12 to 12
- modality: int32 [16384], P('section'), may hold values from 0 to 1
- selected: int32 [16, 256], P('section'), may hold values from 0 to 1023, as said below
- routes: int32 [4096, 1], P('section'), may hold values from 0 to 15, as said below
- norm_gain: float32 [2, 8192], P(None, 'expert'), may hold values from 0.1 to 1.9
- router: float32 [8192], P('expert'), may hold values from -0.0625 to 0.0625
- gate_w: bfloat16 [16, 3072, 8192], P('expert', 'section'), may hold values from -0.0625 to 0.0625
- up_w: bfloat16 [16, 3072, 8192], P('expert', 'section'), may hold values from -0.0625 to 0.0625
- down_w: bfloat16 [16, 3072, 8192], P('expert', 'section'), may hold values from -0.21875 to 0.21875
Outputs:
- block_out: bfloat16 [16384, 8192], P('section', 'expert')
Inputs may be any that keep to these rules, and one draw needn't show every extreme that they name: Each row of selected lists 256 different positions in rising order, the first and the last position among them. `routes`: among the 256 rows of one section group no expert is named more than 24 times, and some expert exactly 24 times; the entry for selected[s, j] is below 8 if that token's modality is 0, and 8 or more if it is 1.
All inputs are finite; a program needn't handle non-finite values.
Results may differ from a plain program's by a relative error of at most 0.0075.
Values may be sent and summed in bfloat16 or wider, within the bound.
No kernel may reach another device: no remote copies, remote signals or barrier semaphores. Data moves between devices by JAX's collectives and lax.ppermute only.
A program may use at most 128 MiB of HBM per device.

v0:
```python
import jax
import jax.numpy as jnp
from jax import lax
from jax.sharding import PartitionSpec as P

EPS = 1e-05


def passed_along(block, axis, distance):
    devices = range(lax.axis_size(axis))
    route = [((i - distance) % len(devices), i) for i in devices]
    return lax.ppermute(block, axis, route)


def feature_product(block, weight):
    return lax.dot_general(
        block, weight, (((1,), (1,)), ((), ())), preferred_element_type=jnp.float32
    )


def slots_of(experts, expert_count):
    onehot = (experts[:, None] == jnp.arange(expert_count, dtype=jnp.int32)[None, :]).astype(
        jnp.int32
    )
    ranks = jnp.cumsum(onehot, axis=0) - 1
    return jnp.sum(ranks * onehot, axis=1)


def body(activations, modality, selected, routes, norm_gain, router, gate_w, up_w, down_w):
    n_section = lax.axis_size("section")
    sel_count = selected.shape[1]
    expert_count = lax.axis_size("expert") * gate_w.shape[0]
    capacity = max(2, 3 * sel_count // (2 * expert_count))
    groups = n_section
    arrived = passed_along(activations, "section", 1)
    sel_next = passed_along(selected, "section", -1)[0]
    routes_next = passed_along(routes, "section", -1)[:, 0]
    rows = activations[sel_next]
    target = routes_next * capacity + slots_of(routes_next, expert_count)
    placing = (
        target[None, :] == jnp.arange(expert_count * capacity, dtype=jnp.int32)[:, None]
    ).astype(jnp.bfloat16)
    feature_width = rows.shape[1]
    buffer = jnp.dot(placing, rows, preferred_element_type=jnp.float32).astype(jnp.bfloat16)
    buffer = buffer.reshape(expert_count, capacity, feature_width)
    n_exp_dev = lax.axis_size("expert")
    local_width = router.shape[0]
    tables = jnp.concatenate([norm_gain, router[None, :]], axis=0)
    parts = []
    rest = tables
    for _ in range(3):
        piece = rest.astype(jnp.bfloat16)
        parts.append(piece)
        rest = rest - piece.astype(jnp.float32)
    table_rows = tables.shape[0]
    extra = jnp.broadcast_to(
        jnp.concatenate(parts, axis=0)[None], (expert_count, 3 * table_rows, local_width)
    )
    buffer = jnp.concatenate([buffer, extra], axis=1)
    mine = lax.all_to_all(buffer, "expert", split_axis=0, concat_axis=2, tiled=True)[0]
    arrived, mine = lax.optimization_barrier((arrived, mine))
    coded = mine[capacity:].astype(jnp.float32).reshape(3, table_rows, mine.shape[1])
    tables = coded[0] + coded[1] + coded[2]
    mine = mine[:capacity]
    gains_all = tables[:2]
    router_all = tables[2]
    expert_id = lax.axis_index("expert")
    kind = (expert_id >= expert_count // 2).astype(jnp.int32)
    gains = lax.dynamic_index_in_dim(gains_all, kind, axis=0, keepdims=False)
    picked = mine.astype(jnp.float32)
    d = picked.shape[1]
    scale = lax.rsqrt(jnp.sum(picked * picked, axis=1) / d + EPS)
    normed = (picked * scale[:, None] * gains[None, :]).astype(jnp.bfloat16)
    score = jax.nn.sigmoid(scale * jnp.sum(picked * gains[None, :] * router_all[None, :], axis=1))
    score_home = passed_along(score, "section", 1)
    half = d // 2
    block_a = lax.all_gather(normed[:, :half], "section", axis=0, tiled=True)
    block_b = lax.all_gather(normed[:, half:], "section", axis=0, tiled=True)
    block_a, score_home = lax.optimization_barrier((block_a, score_home))
    gate = feature_product(block_a, gate_w[0, :, :half]) + feature_product(
        block_b, gate_w[0, :, half:]
    )
    upper = feature_product(block_a, up_w[0, :, :half]) + feature_product(
        block_b, up_w[0, :, half:]
    )
    hidden = (jax.nn.silu(gate) * upper).astype(jnp.bfloat16)
    hidden_width = hidden.shape[1]
    hidden = jnp.roll(hidden.reshape(groups, capacity, hidden_width), 1, axis=0).reshape(
        groups * capacity, hidden_width
    )
    pieces = []
    for columns in (slice(0, half), slice(half, d)):
        part = jnp.dot(hidden, down_w[0, :, columns], preferred_element_type=jnp.float32)
        pieces.append(
            lax.psum_scatter(
                lax.optimization_barrier(part.astype(jnp.bfloat16))
                .astype(jnp.float32)
                .astype(jnp.bfloat16),
                "section",
                scatter_dimension=0,
                tiled=True,
            )
        )
    summed = jnp.concatenate(pieces, axis=1)
    update_rows = (score_home[:, None] * summed.astype(jnp.float32)).astype(jnp.bfloat16)
    outgoing = update_rows.reshape(capacity, n_exp_dev, local_width).transpose(1, 0, 2)
    back = lax.all_to_all(outgoing, "expert", split_axis=0, concat_axis=0, tiled=True)
    flat_back = back.reshape(expert_count * capacity, local_width)
    picks = selected[0]
    experts = routes[:, 0]
    position = experts * capacity + slots_of(experts, expert_count)
    update = flat_back[position].astype(jnp.float32)
    result = arrived.astype(jnp.float32).at[picks].add(update)
    return result.astype(jnp.bfloat16)


def solution(mesh):
    placed = (
        P("section", "expert"),
        P("section"),
        P("section", None),
        P("section", None),
        P(None, "expert"),
        P("expert"),
        P("expert", "section", None),
        P("expert", "section", None),
        P("expert", "section", None),
    )
    return jax.shard_map(
        body, mesh=mesh, in_specs=placed, out_specs=P("section", "expert"), check_vma=False
    )
```

profile of v0, /device:TPU:7, one launch (start us, length us, event | category | flops | bytes accessed | tf_op | source)
XLA Modules:
  0.0 310.3 jit_solution(3256144085192003870)
XLA Ops:
  6.5 0.7 collective-permute-start.1
  7.2 0.3 collective-permute-start.2
  7.5 3.6 %collective-permute-start = (bf16[1024,512]{1,0:T(8,128)(2,1)}, bf16[1024,512]{1,0:T(8,128)(2,1)S(1)}, u32[]{:S(2)}, u32[]{:S(2)}) collective-permute-start(bf16[1024,512]{1,0:T(8,128)(2,1)} %param.9), channel_id=1, source_target_pairs={{240,0},{0,16},{16,32},{32,48},{48,64},{64,80},{80,96},{96,112},{1... | collective-permute-start | bytes 3145736 | tf_op jit(solution)/shard_map/ppermute | solution.py:12
  11.1 0.7 fusion.38
  11.8 0.7 fusion.37
  12.5 0.0 collective-permute-done.1
  12.5 0.6 reduce-window.14
  13.1 0.2 slice_reduce_fusion.1
  13.4 0.1 fusion.34
  13.5 0.0 collective-permute-done.2
  13.5 2.6 gather_fusion
  16.1 0.3 convolution_convert_fusion.2
  16.4 0.9 pad_maximum_fusion
  17.3 10.9 %all-to-all-start = ((bf16[16,33,512]{2,1,0:T(8,128)(2,1)}), bf16[16,33,512]{2,1,0:T(8,128)(2,1)S(1)}, u32[]{:S(2)}, u32[]{:S(2)}) async-start(bf16[16,33,512]{2,1,0:T(8,128)(2,1)} %pad_maximum_fusion), calls=%async_computation | async-start | bytes 1310720 | tf_op jit(solution)/shard_map/all_to_all | solution.py:60
  28.2 0.0 all-gather.3.cloned.1.call-start
  28.3 19.4 %all-to-all-done = bf16[16,33,512]{2,1,0:T(8,128)(2,1)S(1)} async-done(((bf16[16,33,512]{2,1,0:T(8,128)(2,1)}), bf16[16,33,512]{2,1,0:T(8,128)(2,1)S(1)}, u32[]{:S(2)}, u32[]{:S(2)}) %all-to-all-start) | async-done | bytes 540704 | tf_op jit(solution)/shard_map/all_to_all | solution.py:60
  47.6 0.2 copy.34
  47.8 0.1 pad.13
  47.9 0.4 copy.28
  48.3 0.0 collective-permute-done
  48.3 0.0 copy-start.1
  48.3 0.1 slice_add_fusion
  48.5 0.3 fusion.26
  48.8 0.2 fusion.24
  49.0 0.8 fusion.40
  49.8 0.0 all-gather.3.cloned.1.call-update
  49.8 0.0 all-gather.5.cloned.1.call-start
  49.9 0.7 all-gather.5.cloned.1.call-update
  50.6 0.0 reduce-scatter.3.cloned.1.call-start
  50.6 2.0 collective-permute-start.3
  52.6 0.7 collective-permute-done.3
  53.4 29.1 %all-gather.3.cloned.1.call-done = bf16[384,4096]{1,0:T(8,128)(2,1)} async-done(((bf16[24,4096]{1,0:T(8,128)(2,1)}), bf16[384,4096]{1,0:T(8,128)(2,1)}) %all-gather.3.cloned.1.call-update) | async-done | bytes 3145744 | tf_op jit(solution)/shard_map/all_gather | solution.py:77
  82.5 40.4 %all-gather.5.cloned.1.call-done = bf16[384,4096]{1,0:T(8,128)(2,1)} async-done(((bf16[24,4096]{1,0:T(8,128)(2,1)}), bf16[384,4096]{1,0:T(8,128)(2,1)}) %all-gather.5.cloned.1.call-update) | async-done | bytes 3145744 | tf_op jit(solution)/shard_map/all_gather | solution.py:78
  122.9 3.7 %fusion.6 = f32[384,192]{0,1:T(8,128)S(1)} fusion(bf16[384,4096]{1,0:T(8,128)(2,1)} %all-gather.5.cloned.1.call-done, bf16[1,192,8192]{2,1,0:T(8,128)(2,1)} %param.14), kind=kOutput, calls=%fused_computation.11 | convolution fusion | flops 603979776 | bytes 5013504 | tf_op jit(solution)/shard_map/dot_general | solution.py:16
  126.6 0.0 copy-start.6
  126.6 3.2 %fusion.16 = f32[384,192]{0,1:T(8,128)S(1)} fusion(f32[384,192]{0,1:T(8,128)S(1)} %fusion.6, bf16[384,4096]{1,0:T(8,128)(2,1)} %all-gather.3.cloned.1.call-done, bf16[1,192,8192]{2,1,0:T(8,128)(2,1)S(1)} %copy-done.5), kind=kOutput, calls=%fused_computation.25 | convolution fusion | flops 604053504 | bytes 5308416 | tf_op jit(solution)/shard_map/dot_general | solution.py:16
  129.9 0.0 copy-done.8
  129.9 1.2 fusion.2
  131.1 0.7 copy-done.7
  131.8 1.2 multiply_convert_fusion.1
  133.0 0.1 slice_bitcast_fusion
  133.1 0.1 copy.19
  133.3 0.1 copy.20
  133.3 0.1 pad_maximum_fusion.1
  133.4 0.3 copy-done
  133.7 2.7 convolution_convert_fusion.1
  136.4 0.0 reduce-scatter.3.cloned.1.call-update
  136.4 0.0 copy-start.3
  136.4 0.2 reduce-scatter.5.cloned.1.call-start
  136.6 2.6 convolution_convert_fusion
  139.3 0.0 reduce-scatter.5.cloned.1.call-update
  139.3 0.6 reduce-window.16
  139.9 63.1 %reduce-scatter.3.cloned.1.call-done = bf16[24,4096]{1,0:T(8,128)(2,1)} async-done(((bf16[384,4096]{1,0:T(8,128)(2,1)}), bf16[24,4096]{1,0:T(8,128)(2,1)}) %reduce-scatter.3.cloned.1.call-update) | async-done | bytes 196624 | tf_op jit(solution)/shard_map/reduce_scatter | solution.py:95
  203.1 0.9 copy.36
  204.0 67.6 %reduce-scatter.5.cloned.1.call-done = bf16[24,4096]{1,0:T(8,128)(2,1)} async-done(((bf16[384,4096]{1,0:T(8,128)(2,1)}), bf16[24,4096]{1,0:T(8,128)(2,1)}) %reduce-scatter.5.cloned.1.call-update) | async-done | bytes 196624 | tf_op jit(solution)/shard_map/reduce_scatter | solution.py:95
  271.6 0.9 copy.35
  272.6 0.9 fusion.29
  273.5 9.1 %all-to-all-start.1 = ((bf16[16,24,512]{2,1,0:T(8,128)(2,1)}), bf16[16,24,512]{2,1,0:T(8,128)(2,1)S(1)}, u32[]{:S(2)}, u32[]{:S(2)}) async-start(bf16[16,24,512]{2,1,0:T(8,128)(2,1)} %fusion.29), calls=%async_computation.3 | async-start | bytes 786432 | tf_op jit(solution)/shard_map/all_to_all | solution.py:107
  282.6 0.2 slice_reduce_fusion
  282.8 0.1 fusion.32
  283.0 0.3 convert_element_type.78
  283.2 15.4 %all-to-all-done.1 = bf16[16,24,512]{2,1,0:T(8,128)(2,1)S(1)} async-done(((bf16[16,24,512]{2,1,0:T(8,128)(2,1)}), bf16[16,24,512]{2,1,0:T(8,128)(2,1)S(1)}, u32[]{:S(2)}, u32[]{:S(2)}) %all-to-all-start.1) | async-done | bytes 393248 | tf_op jit(solution)/shard_map/all_to_all | solution.py:107
  298.6 4.0 %scatter_custom_fusion = f32[1024,512]{1,0:T(8,128)S(1)} fusion(f32[1024,512]{1,0:T(8,128)S(1)} %convert_element_type.78, s32[256]{0:T(256)S(1)} %bitcast.131, bf16[384,512]{1,0:T(8,128)(2,1)S(1)} %bitcast.110, s32[1024]{0:T(1024)S(1)} %pad_clamp_fusion), kind=kCustom, calls=%fused_computation.35 | custom fusion | flops 262144 | bytes 2494464 | tf_op jit(solution)/shard_map/scatter-add | solution.py:113
  302.7 1.1 convert_element_type.90
  (31 shorter events, 0.3 us)
Async XLA Ops:
  6.5 6.0 %collective-permute-start.1 = (s32[256,1]{0,1:T(1,128)}, s32[256,1]{0,1:T(1,128)S(1)}, u32[]{:S(2)}, u32[]{:S(2)}) collective-permute-start(s32[256,1]{0,1:T(1,128)} %param.11), channel_id=1, source_target_pairs={{16,0},{32,16},{48,32},{64,48},{80,64},{96,80},{112,96},{128,112},... | collective-permute-start | bytes 3080 | tf_op jit(solution)/shard_map/ppermute | solution.py:12
  7.2 6.2 %collective-permute-start.2 = (s32[1,256]{1,0:T(1,128)}, s32[1,256]{1,0:T(1,128)S(1)}, u32[]{:S(2)}, u32[]{:S(2)}) collective-permute-start(s32[1,256]{1,0:T(1,128)} %param.10), channel_id=1, source_target_pairs={{16,0},{32,16},{48,32},{64,48},{80,64},{96,80},{112,96},{128,112},... | collective-permute-start | bytes 3080 | tf_op jit(solution)/shard_map/ppermute | solution.py:12
  7.5 40.8 %collective-permute-start = (bf16[1024,512]{1,0:T(8,128)(2,1)}, bf16[1024,512]{1,0:T(8,128)(2,1)S(1)}, u32[]{:S(2)}, u32[]{:S(2)}) collective-permute-start(bf16[1024,512]{1,0:T(8,128)(2,1)} %param.9), channel_id=1, source_target_pairs={{240,0},{0,16},{16,32},{32,48},{48,64},{64,80},{80,96},{96,112},{1... | collective-permute-start | bytes 3145736 | tf_op jit(solution)/shard_map/ppermute | solution.py:12
  17.3 30.4 %all-to-all-start = ((bf16[16,33,512]{2,1,0:T(8,128)(2,1)}), bf16[16,33,512]{2,1,0:T(8,128)(2,1)S(1)}, u32[]{:S(2)}, u32[]{:S(2)}) async-start(bf16[16,33,512]{2,1,0:T(8,128)(2,1)} %pad_maximum_fusion), calls=%async_computation | async-start | bytes 1310720 | tf_op jit(solution)/shard_map/all_to_all | solution.py:60
  28.2 54.3 %all-gather.3.cloned.1.call-start = ((), (), s32[]{:S(2)}) async-start(), calls=%async_computation.4 | async-start | bytes 3342336 | tf_op jit(solution)/shard_map/all_gather | solution.py:77
  48.3 78.3 %copy-start.1 = (bf16[1024,512]{1,0:T(8,128)(2,1)}, bf16[1024,512]{1,0:T(8,128)(2,1)S(1)}, u32[]{:S(2)}) copy-start(bf16[1024,512]{1,0:T(8,128)(2,1)S(1)} %collective-permute-done) | copy-start | bytes 3145732
  49.8 73.1 %all-gather.5.cloned.1.call-start = ((), (), s32[]{:S(2)}) async-start(), calls=%async_computation.5 | async-start | bytes 3342336 | tf_op jit(solution)/shard_map/all_gather | solution.py:78
  50.6 152.5 %reduce-scatter.3.cloned.1.call-start = ((), (), s32[]{:S(2)}) async-start(), calls=%async_computation.6 | async-start | bytes 3342336 | tf_op jit(solution)/shard_map/reduce_scatter | solution.py:95
  50.6 2.7 collective-permute-start.3
  122.9 3.7 %copy-start.5 = (bf16[1,192,8192]{2,1,0:T(8,128)(2,1)S(1)}, bf16[1,192,8192]{2,1,0:T(8,128)(2,1)}, u32[]{:S(2)}) copy-start(bf16[1,192,8192]{2,1,0:T(8,128)(2,1)} %param.14) | copy-start | bytes 9437188
  122.9 7.0 %copy-start.8 = (bf16[384,4096]{1,0:T(8,128)(2,1)S(1)}, bf16[384,4096]{1,0:T(8,128)(2,1)}, u32[]{:S(2)}) copy-start(bf16[384,4096]{1,0:T(8,128)(2,1)} %all-gather.5.cloned.1.call-done) | copy-start | bytes 9437188
  126.6 3.3 %copy-start.6 = (bf16[1,192,8192]{2,1,0:T(8,128)(2,1)S(1)}, bf16[1,192,8192]{2,1,0:T(8,128)(2,1)}, u32[]{:S(2)}) copy-start(bf16[1,192,8192]{2,1,0:T(8,128)(2,1)} %param.15) | copy-start | bytes 9437188
  129.9 1.9 copy-start.7
  131.8 1.9 copy-start
  136.4 2.9 copy-start.3
  136.4 135.2 %reduce-scatter.5.cloned.1.call-start = ((), (), s32[]{:S(2)}) async-start(), calls=%async_computation.7 | async-start | bytes 3342336 | tf_op jit(solution)/shard_map/reduce_scatter | solution.py:95
  139.3 143.6 %copy-start.4 = (s32[1,256]{1,0:T(1,128)S(1)}, s32[1,256]{1,0:T(1,128)}, u32[]{:S(2)}) copy-start(s32[1,256]{1,0:T(1,128)} %param.10) | copy-start | bytes 3076
  139.3 143.7 %copy-start.2 = (bf16[1024,512]{1,0:T(8,128)(2,1)S(1)}, bf16[1024,512]{1,0:T(8,128)(2,1)}, u32[]{:S(2)}) copy-start(bf16[1024,512]{1,0:T(8,128)(2,1)} %copy-done.1) | copy-start | bytes 3145732
  273.5 25.1 %all-to-all-start.1 = ((bf16[16,24,512]{2,1,0:T(8,128)(2,1)}), bf16[16,24,512]{2,1,0:T(8,128)(2,1)S(1)}, u32[]{:S(2)}, u32[]{:S(2)}) async-start(bf16[16,24,512]{2,1,0:T(8,128)(2,1)} %fusion.29), calls=%async_computation.3 | async-start | bytes 786432 | tf_op jit(solution)/shard_map/all_to_all | solution.py:107
Sparse Core Ops, SparseCore 0:
  49.9 32.5 all-gather.2
  84.3 38.5 all-gather.4
  136.5 66.4 reduce-scatter.2
  205.5 66.1 reduce-scatter.4
where the time goes:
time: 311 us; the launch traced here: 310 us
  waiting for transfers between devices  237 us (76%)
  starting transfers between devices  26.9 us (9%)
  matrix products  14.9 us (5%)
  between operations  13.5 us (4%)
  other arithmetic  10.8 us (3%)
  local copies, waits for them, and re-layouts  7.66 us (2%)
    reduce_scatter x2, waiting for transfers between devices, body(): lax.psum_scatter(lax.optimization_barrier(part.astype(jnp.bfloat16)).asty...  131 us
    all_gather x1, waiting for transfers between devices, body(): block_b = lax.all_gather(normed[:, half:], 'section', axis=0, tiled=True)  40.4 us
    all_gather x1, waiting for transfers between devices, body(): block_a = lax.all_gather(normed[:, :half], 'section', axis=0, tiled=True)  29.1 us
    all_to_all x1, waiting for transfers between devices, body(): lax.all_to_all(buffer, 'expert', split_axis=0, concat_axis=2, tiled=True)[0]  19.4 us
    all_to_all x1, waiting for transfers between devices, body(): lax.all_to_all(outgoing, 'expert', split_axis=0, concat_axis=0, tiled=True)  15.4 us
    all_to_all x1, starting transfers between devices, body(): lax.all_to_all(buffer, 'expert', split_axis=0, concat_axis=2, tiled=True)[0]  10.9 us
    dot_general x4, matrix products, feature_product(): lax.dot_general(block, weight, (((1,), (1,)), ((), ())), preferred_elemen...  9.33 us
    all_to_all x1, starting transfers between devices, body(): lax.all_to_all(outgoing, 'expert', split_axis=0, concat_axis=0, tiled=True)  9.06 us
  transfers between devices with their start and end apart: 10, of which 7 were waited for; matrix products, arithmetic and copies ran while one was open for 4% of the time, Pallas kernels for 0%

commit v1 on v0

--- a/solution.py
+++ b/solution.py
@@ -74,7 +74,9 @@
     score = jax.nn.sigmoid(scale * jnp.sum(picked * gains[None, :] * router_all[None, :], axis=1))
     score_home = passed_along(score, "section", 1)
     half = d // 2
-    block_a = lax.all_gather(normed[:, :half], "section", axis=0, tiled=True)
+    x = normed[:, :half]
+    outgoing_2 = jnp.stack([x] * lax.axis_size("section"))
+    block_a = jnp.concatenate(lax.all_to_all(outgoing_2, "section", 0, 0), axis=0)
     block_b = lax.all_gather(normed[:, half:], "section", axis=0, tiled=True)
     block_a, score_home = lax.optimization_barrier((block_a, score_home))
     gate = feature_product(block_a, gate_w[0, :, :half]) + feature_product(

time: 311 us -> 297 us (0.955)
  waiting for transfers between devices: 237 us -> 216 us
  starting transfers between devices: 26.9 us -> 32.3 us
    all_gather x1, waiting for transfers between devices: 40.4 us -> 5.64 us  [body(): block_b = lax.all_gather(normed[:, half:], 'section', axis=0, tiled=True)]
    all_gather x1 -> x0, waiting for transfers between devices: 29.1 us -> none  [body(): block_a = lax.all_gather(normed[:, :half], 'section', axis=0, tiled=True)]
    ppermute x4, waiting for transfers between devices: 0.73 us -> 27 us  [passed_along(): return lax.ppermute(block, axis, route)]
    all_to_all x0 -> x1, waiting for transfers between devices: none -> 19.2 us  [body(): lax.all_to_all(outgoing_2, 'section', 0, 0)]
    all_to_all x0 -> x1, starting transfers between devices: none -> 5.97 us  [body(): lax.all_to_all(outgoing_2, 'section', 0, 0)]
  transfers between devices with their start and end apart: 10 -> 10, of which waited for: 7 -> 7; matrix products, arithmetic and copies ran while one was open for 4% -> 5% of each run, Pallas kernels for 0% -> 0%
where the time goes in v1:
time: 297 us
  waiting for transfers between devices  216 us (73%)
  starting transfers between devices  32.3 us (11%)
  matrix products  14.5 us (5%)
  between operations  13.4 us (5%)
  other arithmetic  10.8 us (4%)
  local copies, waits for them, and re-layouts  9.43 us (3%)
    reduce_scatter x2, waiting for transfers between devices, body(): lax.psum_scatter(lax.optimization_barrier(part.astype(jnp.bfloat16)).asty...  129 us
    ppermute x4, waiting for transfers between devices, passed_along(): return lax.ppermute(block, axis, route)  27 us
    all_to_all x1, waiting for transfers between devices, body(): lax.all_to_all(buffer, 'expert', split_axis=0, concat_axis=2, tiled=True)[0]  19.4 us
    all_to_all x1, waiting for transfers between devices, body(): lax.all_to_all(outgoing_2, 'section', 0, 0)  19.2 us
    all_to_all x1, waiting for transfers between devices, body(): lax.all_to_all(outgoing, 'expert', split_axis=0, concat_axis=0, tiled=True)  15.4 us
    all_to_all x1, starting transfers between devices, body(): lax.all_to_all(buffer, 'expert', split_axis=0, concat_axis=2, tiled=True)[0]  10.9 us
    all_to_all x1, starting transfers between devices, body(): lax.all_to_all(outgoing, 'expert', split_axis=0, concat_axis=0, tiled=True)  9.03 us
    dot_general x4, matrix products, feature_product(): lax.dot_general(block, weight, (((1,), (1,)), ((), ())), preferred_elemen...  7.3 us
  transfers between devices with their start and end apart: 10, of which 7 were waited for; matrix products, arithmetic and copies ran while one was open for 5% of the time, Pallas kernels for 0%

profile of v1, /device:TPU:7, one launch (start us, length us, event | category | flops | bytes accessed | tf_op | source)
XLA Modules:
  0.0 296.6 jit_solution(16365952748406818884)
XLA Ops:
  6.5 0.7 collective-permute-start.1
  7.2 0.3 collective-permute-start.2
  7.5 3.6 %collective-permute-start = (bf16[1024,512]{1,0:T(8,128)(2,1)}, bf16[1024,512]{1,0:T(8,128)(2,1)S(1)}, u32[]{:S(2)}, u32[]{:S(2)}) collective-permute-start(bf16[1024,512]{1,0:T(8,128)(2,1)} %param.9), channel_id=1, source_target_pairs={{240,0},{0,16},{16,32},{32,48},{48,64},{64,80},{80,96},{96,112},{1... | collective-permute-start | bytes 3145736 | tf_op jit(solution)/shard_map/ppermute | solution.py:12
  11.1 0.7 fusion.38
  11.8 0.7 fusion.37
  12.5 0.0 collective-permute-done.1
  12.5 0.6 reduce-window.14
  13.1 0.2 slice_reduce_fusion.1
  13.4 0.1 fusion.34
  13.5 0.0 collective-permute-done.2
  13.5 2.6 gather_fusion
  16.1 0.3 convolution_convert_fusion.2
  16.4 0.9 pad_maximum_fusion
  17.3 10.9 %all-to-all-start = ((bf16[16,33,512]{2,1,0:T(8,128)(2,1)}), bf16[16,33,512]{2,1,0:T(8,128)(2,1)S(1)}, u32[]{:S(2)}, u32[]{:S(2)}) async-start(bf16[16,33,512]{2,1,0:T(8,128)(2,1)} %pad_maximum_fusion), calls=%async_computation | async-start | bytes 1310720 | tf_op jit(solution)/shard_map/all_to_all | solution.py:60
  28.2 0.0 all-gather.2.cloned.1.call-start
  28.2 19.4 %all-to-all-done = bf16[16,33,512]{2,1,0:T(8,128)(2,1)S(1)} async-done(((bf16[16,33,512]{2,1,0:T(8,128)(2,1)}), bf16[16,33,512]{2,1,0:T(8,128)(2,1)S(1)}, u32[]{:S(2)}, u32[]{:S(2)}) %all-to-all-start) | async-done | bytes 540704 | tf_op jit(solution)/shard_map/all_to_all | solution.py:60
  47.6 0.2 copy.34
  47.8 0.1 pad.13
  47.9 0.4 copy.28
  48.3 0.0 collective-permute-done
  48.3 0.0 copy-start.1
  48.3 0.1 slice_add_fusion
  48.5 0.3 fusion.26
  48.8 0.2 fusion.24
  49.0 0.7 fusion.40
  49.7 0.0 all-gather.2.cloned.1.call-update
  49.7 2.1 stack.2
  51.8 0.0 copy-done.1
  51.8 6.0 %all-to-all-start.1 = ((bf16[16,24,4096]{2,1,0:T(8,128)(2,1)}), bf16[16,24,4096]{2,1,0:T(8,128)(2,1)S(1)}, u32[]{:S(2)}, u32[]{:S(2)}) async-start(bf16[16,24,4096]{2,1,0:T(8,128)(2,1)} %stack.2), calls=%async_computation.1 | async-start | bytes 6291456 | tf_op jit(solution)/shard_map/all_to_all | solution.py:79
  57.8 0.0 reduce-scatter.5.cloned.1.call-start
  57.8 1.5 collective-permute-start.3
  59.3 27.0 %collective-permute-done.3 = f32[24]{0:T(128)S(1)} collective-permute-done((f32[24]{0:T(128)S(1)}, f32[24]{0:T(128)S(1)}, u32[]{:S(2)}, u32[]{:S(2)}) %collective-permute-start.3) | collective-permute-done | bytes 128 | tf_op jit(solution)/shard_map/ppermute | solution.py:12
  86.3 19.2 %all-to-all-done.1 = bf16[16,24,4096]{2,1,0:T(8,128)(2,1)S(1)} async-done(((bf16[16,24,4096]{2,1,0:T(8,128)(2,1)}), bf16[16,24,4096]{2,1,0:T(8,128)(2,1)S(1)}, u32[]{:S(2)}, u32[]{:S(2)}) %all-to-all-start.1) | async-done | bytes 3145760 | tf_op jit(solution)/shard_map/all_to_all | solution.py:79
  105.5 5.6 %all-gather.2.cloned.1.call-done = bf16[384,4096]{1,0:T(8,128)(2,1)} async-done(((bf16[24,4096]{1,0:T(8,128)(2,1)}), bf16[384,4096]{1,0:T(8,128)(2,1)}) %all-gather.2.cloned.1.call-update) | async-done | bytes 3145744 | tf_op jit(solution)/shard_map/all_gather | solution.py:80
  111.2 3.7 %fusion.6 = f32[384,192]{0,1:T(8,128)S(1)} fusion(bf16[384,4096]{1,0:T(8,128)(2,1)} %all-gather.2.cloned.1.call-done, bf16[1,192,8192]{2,1,0:T(8,128)(2,1)} %param.14), kind=kOutput, calls=%fused_computation.11 | convolution fusion | flops 603979776 | bytes 5013504 | tf_op jit(solution)/shard_map/dot_general | solution.py:16
  114.9 0.0 copy-start.6
  114.9 1.2 fusion.16
  116.1 0.8 copy-done.6
  116.9 1.2 fusion.2
  118.1 1.2 multiply_convert_fusion.1
  119.3 0.1 slice_bitcast_fusion
  119.4 0.1 copy.19
  119.6 0.1 copy.20
  119.6 0.1 pad_maximum_fusion.1
  119.7 0.0 copy-start
  119.7 4.2 %convolution_convert_fusion = bf16[384,4096]{1,0:T(8,128)(2,1)} fusion(bf16[384,192]{1,0:T(8,128)(2,1)S(1)} %bitcast.108, bf16[1,192,8192]{2,1,0:T(8,128)(2,1)} %param.16), kind=kOutput, calls=%fused_computation.3 | convolution fusion | flops 605552640 | bytes 4866048 | tf_op jit(solution)/shard_map/dot_general | solution.py:95
  123.9 0.0 reduce-scatter.5.cloned.1.call-update
  123.9 0.0 copy-start.3
  123.9 0.2 reduce-scatter.3.cloned.1.call-start
  124.2 2.7 convolution_convert_fusion.1
  126.9 0.0 reduce-scatter.3.cloned.1.call-update
  126.9 0.6 reduce-window.16
  127.5 61.7 %reduce-scatter.5.cloned.1.call-done = bf16[24,4096]{1,0:T(8,128)(2,1)} async-done(((bf16[384,4096]{1,0:T(8,128)(2,1)}), bf16[24,4096]{1,0:T(8,128)(2,1)}) %reduce-scatter.5.cloned.1.call-update) | async-done | bytes 196624 | tf_op jit(solution)/shard_map/reduce_scatter | solution.py:97
  189.2 0.9 copy.35
  190.1 67.8 %reduce-scatter.3.cloned.1.call-done = bf16[24,4096]{1,0:T(8,128)(2,1)} async-done(((bf16[384,4096]{1,0:T(8,128)(2,1)}), bf16[24,4096]{1,0:T(8,128)(2,1)}) %reduce-scatter.3.cloned.1.call-update) | async-done | bytes 196624 | tf_op jit(solution)/shard_map/reduce_scatter | solution.py:97
  257.9 0.9 copy.36
  258.9 0.9 fusion.29
  259.8 9.0 %all-to-all-start.2 = ((bf16[16,24,512]{2,1,0:T(8,128)(2,1)}), bf16[16,24,512]{2,1,0:T(8,128)(2,1)S(1)}, u32[]{:S(2)}, u32[]{:S(2)}) async-start(bf16[16,24,512]{2,1,0:T(8,128)(2,1)} %fusion.29), calls=%async_computation.4 | async-start | bytes 786432 | tf_op jit(solution)/shard_map/all_to_all | solution.py:109
  268.9 0.2 slice_reduce_fusion
  269.1 0.1 fusion.32
  269.2 0.3 convert_element_type.78
  269.5 15.4 %all-to-all-done.2 = bf16[16,24,512]{2,1,0:T(8,128)(2,1)S(1)} async-done(((bf16[16,24,512]{2,1,0:T(8,128)(2,1)}), bf16[16,24,512]{2,1,0:T(8,128)(2,1)S(1)}, u32[]{:S(2)}, u32[]{:S(2)}) %all-to-all-start.2) | async-done | bytes 393248 | tf_op jit(solution)/shard_map/all_to_all | solution.py:109
  284.9 4.0 %scatter_custom_fusion = f32[1024,512]{1,0:T(8,128)S(1)} fusion(f32[1024,512]{1,0:T(8,128)S(1)} %convert_element_type.78, s32[256]{0:T(256)S(1)} %bitcast.134, bf16[384,512]{1,0:T(8,128)(2,1)S(1)} %bitcast.113, s32[1024]{0:T(1024)S(1)} %pad_clamp_fusion), kind=kCustom, calls=%fused_computation.35 | custom fusion | flops 262144 | bytes 2494464 | tf_op jit(solution)/shard_map/scatter-add | solution.py:115
  288.9 1.1 convert_element_type.90
  (29 shorter events, 0.3 us)
Async XLA Ops:
  6.5 6.0 %collective-permute-start.1 = (s32[256,1]{0,1:T(1,128)}, s32[256,1]{0,1:T(1,128)S(1)}, u32[]{:S(2)}, u32[]{:S(2)}) collective-permute-start(s32[256,1]{0,1:T(1,128)} %param.11), channel_id=1, source_target_pairs={{16,0},{32,16},{48,32},{64,48},{80,64},{96,80},{112,96},{128,112},... | collective-permute-start | bytes 3080 | tf_op jit(solution)/shard_map/ppermute | solution.py:12
  7.2 6.2 %collective-permute-start.2 = (s32[1,256]{1,0:T(1,128)}, s32[1,256]{1,0:T(1,128)S(1)}, u32[]{:S(2)}, u32[]{:S(2)}) collective-permute-start(s32[1,256]{1,0:T(1,128)} %param.10), channel_id=1, source_target_pairs={{16,0},{32,16},{48,32},{64,48},{80,64},{96,80},{112,96},{128,112},... | collective-permute-start | bytes 3080 | tf_op jit(solution)/shard_map/ppermute | solution.py:12
  7.5 40.8 %collective-permute-start = (bf16[1024,512]{1,0:T(8,128)(2,1)}, bf16[1024,512]{1,0:T(8,128)(2,1)S(1)}, u32[]{:S(2)}, u32[]{:S(2)}) collective-permute-start(bf16[1024,512]{1,0:T(8,128)(2,1)} %param.9), channel_id=1, source_target_pairs={{240,0},{0,16},{16,32},{32,48},{48,64},{64,80},{80,96},{96,112},{1... | collective-permute-start | bytes 3145736 | tf_op jit(solution)/shard_map/ppermute | solution.py:12
  17.3 30.4 %all-to-all-start = ((bf16[16,33,512]{2,1,0:T(8,128)(2,1)}), bf16[16,33,512]{2,1,0:T(8,128)(2,1)S(1)}, u32[]{:S(2)}, u32[]{:S(2)}) async-start(bf16[16,33,512]{2,1,0:T(8,128)(2,1)} %pad_maximum_fusion), calls=%async_computation | async-start | bytes 1310720 | tf_op jit(solution)/shard_map/all_to_all | solution.py:60
  28.2 83.0 %all-gather.2.cloned.1.call-start = ((), (), s32[]{:S(2)}) async-start(), calls=%async_computation.5 | async-start | bytes 3342336 | tf_op jit(solution)/shard_map/all_gather | solution.py:80
  48.3 3.5 %copy-start.1 = (bf16[1024,512]{1,0:T(8,128)(2,1)}, bf16[1024,512]{1,0:T(8,128)(2,1)S(1)}, u32[]{:S(2)}) copy-start(bf16[1024,512]{1,0:T(8,128)(2,1)S(1)} %collective-permute-done) | copy-start | bytes 3145732
  51.8 53.7 %all-to-all-start.1 = ((bf16[16,24,4096]{2,1,0:T(8,128)(2,1)}), bf16[16,24,4096]{2,1,0:T(8,128)(2,1)S(1)}, u32[]{:S(2)}, u32[]{:S(2)}) async-start(bf16[16,24,4096]{2,1,0:T(8,128)(2,1)} %stack.2), calls=%async_computation.1 | async-start | bytes 6291456 | tf_op jit(solution)/shard_map/all_to_all | solution.py:79
  57.8 131.4 %reduce-scatter.5.cloned.1.call-start = ((), (), s32[]{:S(2)}) async-start(), calls=%async_computation.7 | async-start | bytes 3342336 | tf_op jit(solution)/shard_map/reduce_scatter | solution.py:97
  57.8 28.5 %collective-permute-start.3 = (f32[24]{0:T(128)S(1)}, f32[24]{0:T(128)S(1)}, u32[]{:S(2)}, u32[]{:S(2)}) collective-permute-start(f32[24]{0:T(128)S(1)} %get-tuple-element.19), channel_id=1, source_target_pairs={{240,0},{0,16},{16,32},{32,48},{48,64},{64,80},{80,96},{96,112},{1... | collective-permute-start | bytes 296 | tf_op jit(solution)/shard_map/ppermute | solution.py:12
  111.2 3.7 %copy-start.5 = (bf16[1,192,8192]{2,1,0:T(8,128)(2,1)S(1)}, bf16[1,192,8192]{2,1,0:T(8,128)(2,1)}, u32[]{:S(2)}) copy-start(bf16[1,192,8192]{2,1,0:T(8,128)(2,1)} %param.14) | copy-start | bytes 9437188
  111.2 4.9 %copy-start.7 = (bf16[384,4096]{1,0:T(8,128)(2,1)S(1)}, bf16[384,4096]{1,0:T(8,128)(2,1)}, u32[]{:S(2)}) copy-start(bf16[384,4096]{1,0:T(8,128)(2,1)} %all-gather.2.cloned.1.call-done) | copy-start | bytes 9437188
  114.9 2.0 copy-start.6
  119.7 4.5 %copy-start = (bf16[1,192,8192]{2,1,0:T(8,128)(2,1)S(1)}, bf16[1,192,8192]{2,1,0:T(8,128)(2,1)}, u32[]{:S(2)}) copy-start(bf16[1,192,8192]{2,1,0:T(8,128)(2,1)} %param.16) | copy-start | bytes 9437188
  123.9 3.0 %copy-start.3 = (s32[256,1]{0,1:T(1,128)S(1)}, s32[256,1]{0,1:T(1,128)}, u32[]{:S(2)}) copy-start(s32[256,1]{0,1:T(1,128)} %param.11) | copy-start | bytes 3076
  123.9 134.0 %reduce-scatter.3.cloned.1.call-start = ((), (), s32[]{:S(2)}) async-start(), calls=%async_computation.6 | async-start | bytes 3342336 | tf_op jit(solution)/shard_map/reduce_scatter | solution.py:97
  126.9 142.3 %copy-start.4 = (s32[1,256]{1,0:T(1,128)S(1)}, s32[1,256]{1,0:T(1,128)}, u32[]{:S(2)}) copy-start(s32[1,256]{1,0:T(1,128)} %param.10) | copy-start | bytes 3076
  126.9 142.4 %copy-start.2 = (bf16[1024,512]{1,0:T(8,128)(2,1)S(1)}, bf16[1024,512]{1,0:T(8,128)(2,1)}, u32[]{:S(2)}) copy-start(bf16[1024,512]{1,0:T(8,128)(2,1)} %copy-done.1) | copy-start | bytes 3145732
  259.8 25.1 %all-to-all-start.2 = ((bf16[16,24,512]{2,1,0:T(8,128)(2,1)}), bf16[16,24,512]{2,1,0:T(8,128)(2,1)S(1)}, u32[]{:S(2)}, u32[]{:S(2)}) async-start(bf16[16,24,512]{2,1,0:T(8,128)(2,1)} %fusion.29), calls=%async_computation.4 | async-start | bytes 786432 | tf_op jit(solution)/shard_map/all_to_all | solution.py:109
Sparse Core Ops, SparseCore 0:
  49.8 61.2 all-gather.1
  124.0 65.0 reduce-scatter.4
  191.7 66.1 reduce-scatter.2
